TPU v7x, 32 devices: a whole 2x2x4 slice. The times are simulated.
32 devices in a mesh: groups: 2 (over y), seq: 4 (over z), tensor: 4 (over x, core).
Axes of the slice: x: 2, y: 2, z: 4, core: 2. Of those that a mesh axis runs over, the one named last changes fastest.
Arguments:
- x_in: bfloat16 [4096, 5120], P(('groups', 'seq'), 'tensor'), parts along dimension 0, may hold values from -6 to 6
- z_gate: bfloat16 [4096, 5120], P(('groups', 'seq'), 'tensor'), parts along dimension 0, may hold values from -32 to 32
- bc_in: bfloat16 [4096, 256], P(('groups', 'seq')), parts along dimension 0, may hold values from -6 to 6
- step_size: float32 [80, 4096], P('tensor', ('groups', 'seq')), parts along dimension 1, may hold values from 0 to 0.4
- log_keep: float32 [80, 4096], P('tensor', ('groups', 'seq')), parts along dimension 1, may hold values from -1 to 0
- skip_gain: float32 [80], P('tensor'), may hold values from 0.5 to 2
- conv_x: bfloat16 [4, 5120], P(None, 'tensor'), may hold values from -3 to 3
- conv_bc: bfloat16 [4, 256], replicated, may hold values from -3 to 3
- norm_gain: float32 [5120], P('tensor'), may hold values from 0.1 to 1.9
- seg_ends: int32 [1024], P(('groups', 'seq')), parts along dimension 0, may hold values from 0 to 2047, as said below
- pool_query: bfloat16 [320, 5120], P(('groups', 'seq'), 'tensor'), parts along dimension 0, may hold values from -64 to 64
- pool_start: int32 [320], P(('groups', 'seq')), parts along dimension 0, may hold values from 0 to 255, as said below
- pool_stop: int32 [320], P(('groups', 'seq')), parts along dimension 0, may hold values from 64 to 512
Outputs:
- mixed_seq: bfloat16 [4096, 5120], P(('groups', 'seq'), 'tensor'), parts along dimension 0
- pooled: float32 [320, 5120], P(('groups', 'seq'), 'tensor'), parts along dimension 0
There are 2 independent parts, one for each index of `groups`. A program takes and returns all parts, laid end to end along the dimension named above; an argument that names none is the same for every part. Nothing has to cross between parts.
Inputs may be any that keep to these rules, and one draw needn't show every extreme that they name: The tokens fall into blocks of 512; block b holds exactly the 128 segment ends seg_ends[b * 128] to seg_ends[(b + 1) * 128 - 1], strictly increasing. pool_start < pool_stop for every pooled row.
All inputs are finite; a program needn't handle non-finite values.
Results may differ from a plain program's by a relative error of at most 0.039.
Values may be sent and summed in bfloat16 or wider, within the bound.
No kernel may reach another device: no remote copies, remote signals or barrier semaphores. Data moves between devices by JAX's collectives and lax.ppermute only.
A program may use at most 64 MiB of HBM per device.

v0:
```python
import math
import jax
import jax.numpy as jnp
from jax import lax
from jax.sharding import PartitionSpec as P

STRETCH = 256
POOL_HEADS = 32
EPSILON = 1e-05
MASKED = -1e30


def passed_along(value, axis, steps):
    count = lax.axis_size(axis)
    leading, last = (max(0, -steps), min(count, count - steps))
    return lax.ppermute(value, axis, [(source, source + steps) for source in range(leading, last)])


def prefix(part, axis, combine, identity):
    place = lax.axis_index(axis)
    gathered = jax.tree.map(lambda a: lax.all_gather(a, axis), part)
    state = jax.tree.map(lambda a, e: jnp.zeros_like(a) + jnp.asarray(e, a.dtype), part, identity)

    def one(lap, state):
        return combine(
            state, jax.tree.map(lambda a: lax.dynamic_index_in_dim(a, lap, 0, False), gathered)
        )

    return lax.fori_loop(0, place, one, state)


def silu_act(values):
    return values / (1.0 + jnp.exp(-values))


def causal_conv(before, current, weights):
    kernel_width = weights.shape[0]
    length = current.shape[0]
    padded = jnp.concatenate([before, current], axis=0)
    summed = jnp.zeros(current.shape, jnp.float32)
    for offset in range(kernel_width):
        summed = summed + padded[offset : offset + length].astype(jnp.float32) * weights[
            offset
        ].astype(jnp.float32)
    return silu_act(summed).astype(jnp.bfloat16)


def stretch_local(x_block, b_block, c_block, step_block, keep_block):
    block_len = x_block.shape[0]
    cumul_keep = jnp.cumsum(keep_block, axis=1)
    lower_mask = lax.broadcasted_iota(jnp.int32, (block_len, block_len), 0) >= lax.broadcasted_iota(
        jnp.int32, (block_len, block_len), 1
    )
    inner_prod = jnp.einsum("is,js->ij", c_block, b_block, preferred_element_type=jnp.float32)
    spread = cumul_keep[:, :, None] - cumul_keep[:, None, :]
    decay_mask = jnp.where(lower_mask[None], jnp.exp(jnp.where(lower_mask[None], spread, 0.0)), 0.0)
    mixing = (decay_mask * inner_prod[None] * step_block[:, None, :]).astype(jnp.bfloat16)
    intra_part = jnp.einsum("hij,jhp->ihp", mixing, x_block, preferred_element_type=jnp.float32)
    tail_weight = jnp.exp(cumul_keep[:, -1:] - cumul_keep) * step_block
    weighted = (tail_weight.T[:, :, None] * x_block.astype(jnp.float32)).astype(jnp.bfloat16)
    stretch_state = jnp.einsum("jhp,js->hps", weighted, b_block, preferred_element_type=jnp.float32)
    return (intra_part, stretch_state, cumul_keep)


def combine(earlier, later):
    return (earlier[0] * jnp.exp(later[1])[:, None, None] + later[0], earlier[1] + later[1])


def read_state(c_block, state_in):
    state_high = state_in.astype(jnp.bfloat16)
    state_low = (state_in - state_high.astype(jnp.float32)).astype(jnp.bfloat16)
    high_part = jnp.einsum("is,hps->ihp", c_block, state_high, preferred_element_type=jnp.float32)
    low_part = jnp.einsum("is,hps->ihp", c_block, state_low, preferred_element_type=jnp.float32)
    return high_part + low_part


def local(
    x_in,
    z_gate,
    bc_in,
    step_size,
    log_keep,
    skip_gain,
    conv_x,
    conv_bc,
    norm_gain,
    seg_ends,
    pool_query,
    pool_start,
    pool_stop,
):
    tok_rows = x_in.shape[0]
    channels = x_in.shape[1]
    heads_local = step_size.shape[0]
    head_width = channels // heads_local
    state_width = bc_in.shape[1] // 2
    rim_rows = conv_x.shape[0] - 1
    edge_rows = jnp.concatenate([x_in[tok_rows - rim_rows :], bc_in[tok_rows - rim_rows :]], axis=1)
    before = passed_along(edge_rows, "seq", 1)
    x_conv = causal_conv(before[:, :channels], x_in, conv_x)
    bc_conv = causal_conv(before[:, channels:], bc_in, conv_bc)
    b_mat = bc_conv[:, :state_width]
    c_mat = bc_conv[:, state_width:]
    x_heads = x_conv.reshape(tok_rows, heads_local, head_width)
    stretch_count = tok_rows // STRETCH
    entry_state = jnp.zeros((heads_local, head_width, state_width), jnp.float32)
    decay_total = jnp.zeros((heads_local,), jnp.float32)
    saved_parts = []
    for block_index in range(stretch_count):
        first_row = block_index * STRETCH
        last_row = first_row + STRETCH
        intra_part, stretch_state, cumul_keep = stretch_local(
            x_heads[first_row:last_row],
            b_mat[first_row:last_row],
            c_mat[first_row:last_row],
            step_size[:, first_row:last_row],
            log_keep[:, first_row:last_row],
        )
        saved_parts.append((intra_part, cumul_keep, entry_state, decay_total))
        entry_state = jnp.exp(cumul_keep[:, -1])[:, None, None] * entry_state + stretch_state
        decay_total = decay_total + cumul_keep[:, -1]
    incoming, unused = prefix(
        (entry_state, decay_total),
        "seq",
        combine,
        (jnp.zeros_like(entry_state), jnp.zeros_like(decay_total)),
    )
    pieces_out = []
    for block_index in range(stretch_count):
        intra_part, cumul_keep, entry_part, decay_part = saved_parts[block_index]
        first_row = block_index * STRETCH
        state_in = entry_part + jnp.exp(decay_part)[:, None, None] * incoming
        from_state = read_state(c_mat[first_row : first_row + STRETCH], state_in)
        pieces_out.append(intra_part + jnp.exp(cumul_keep).T[:, :, None] * from_state)
    ssd_out = jnp.concatenate(pieces_out, axis=0) + skip_gain[None, :, None] * x_heads.astype(
        jnp.float32
    )
    gated = ssd_out.reshape(tok_rows, channels) * silu_act(z_gate.astype(jnp.float32))
    square_sum = lax.psum(jnp.sum(gated * gated, axis=1), "tensor")
    width_all = channels * lax.axis_size("tensor")
    mixed_seq = (
        gated * lax.rsqrt(square_sum / width_all + EPSILON)[:, None] * norm_gain[None, :]
    ).astype(jnp.bfloat16)
    local_ends = seg_ends - lax.axis_index("seq") * tok_rows
    summaries = jnp.take(mixed_seq, local_ends, axis=0)
    pool_heads_local = POOL_HEADS // lax.axis_size("tensor")
    pool_width = channels // pool_heads_local
    scale_factor = 1.0 / math.sqrt(pool_width)
    pools_local = pool_query.shape[0]
    queries = pool_query.reshape(pools_local, pool_heads_local, pool_width)
    piece = lax.all_gather(summaries, "seq", axis=0, tiled=True)
    peak = jnp.full((pool_heads_local, pools_local), MASKED, jnp.float32)
    numer = jnp.zeros((pools_local, pool_heads_local, pool_width), jnp.float32)
    count = piece.shape[0]
    seg_index = lax.iota(jnp.int32, count)
    inside = (seg_index[None, :] >= pool_start[:, None]) & (seg_index[None, :] < pool_stop[:, None])
    keys_block = piece.reshape(count, pool_heads_local, pool_width)
    logits = (
        jnp.einsum("pad,rad->apr", queries, keys_block, preferred_element_type=jnp.float32)
        * scale_factor
    )
    logits = jnp.where(inside[None], logits, MASKED)
    new_peak = jnp.maximum(peak, jnp.max(logits, axis=2))
    expo = jnp.where(inside[None], jnp.exp(logits - new_peak[:, :, None]), 0.0)
    rescale = jnp.exp(peak - new_peak)
    denom = jnp.sum(expo, axis=2)
    numer = numer * rescale.T[:, :, None] + jnp.einsum(
        "apr,rad->pad", expo.astype(jnp.bfloat16), keys_block, preferred_element_type=jnp.float32
    )
    peak, denom, numer = (new_peak, denom, numer)
    pooled = (numer / denom.T[:, :, None]).reshape(pools_local, channels)
    return (mixed_seq, pooled)


def solution(mesh):
    in_specs = (
        P(("groups", "seq"), "tensor"),
        P(("groups", "seq"), "tensor"),
        P(("groups", "seq"), None),
        P("tensor", ("groups", "seq")),
        P("tensor", ("groups", "seq")),
        P("tensor"),
        P(None, "tensor"),
        P(),
        P("tensor"),
        P(("groups", "seq")),
        P(("groups", "seq"), "tensor"),
        P(("groups", "seq")),
        P(("groups", "seq")),
    )
    out_specs = (P(("groups", "seq"), "tensor"), P(("groups", "seq"), "tensor"))
    return jax.shard_map(local, mesh=mesh, in_specs=in_specs, out_specs=out_specs, check_vma=False)
```

profile of v0, /device:TPU:0, one launch (start us, length us, event | category | flops | bytes accessed | tf_op | source)
XLA Modules:
  0.0 157.4 jit_solution(5044019205403970520)
XLA Ops:
  7.2 0.7 slice.120
  7.9 0.7 slice.121
  8.7 5.0 %collective-permute-start = (bf16[3,1536]{1,0:T(4,128)(2,1)S(1)}, bf16[3,1536]{1,0:T(4,128)(2,1)S(1)}, u32[]{:S(2)}, u32[]{:S(2)}) collective-permute-start(bf16[3,1536]{1,0:T(4,128)(2,1)S(1)} %pad_maximum_fusion.2), channel_id=1, source_target_pairs={{0,4},{4,8},{8,12},{1,5},{5,9},{9,13},{2,6},{6,10},{10,14},{3,7},{... | collective-permute-start | bytes 27656 | tf_op jit(solution)/shard_map/ppermute | solution.py:16
  13.6 0.8 fusion.71
  14.4 0.6 reduce-window.14
  15.4 0.6 reduce-window.16
  16.3 0.8 slice_convert_fusion.3
  17.2 0.8 slice_reduce_fusion.2
  17.9 0.5 fusion.72
  18.5 1.5 fusion.70
  19.9 0.9 convert_reduce_fusion.3
  20.8 0.6 exp.65
  21.5 4.0 %divide_convert_fusion = bf16[512,1280]{1,0:T(8,128)(2,1)S(1)} fusion(bf16[512,1280]{1,0:T(8,128)(2,1)} %param.15, bf16[3,1280]{1,0:T(4,128)(2,1)S(1)} %slice.158, f32[1280]{0:T(1024)S(1)} %get-tuple-element.52, f32[1280]{0:T(1024)S(1)} %get-tuple-element.53, f32[1280]{0:T(1024)S(1)} %get-tuple-element.51, f32[1280]{0:T(1024)S(1)} %get-tuple-element.50), kind=kLoop, calls=%fused_computation.25 | loop fusion | flops 15728640 | bytes 2649600 | tf_op jit(solution)/shard_map/convert_element_type | solution.py:45
  25.6 0.2 copy.34
  25.8 0.2 copy.39
  26.1 1.9 %divide_convert_fusion.1 = bf16[512,256]{1,0:T(8,128)(2,1)S(1)} fusion(bf16[512,256]{1,0:T(8,128)(2,1)} %param.17, bf16[3,256]{1,0:T(4,128)(2,1)S(1)} %slice.165, f32[256]{0:T(256)S(1)} %bitcast.90, f32[256]{0:T(256)S(1)} %bitcast.91, f32[256]{0:T(256)S(1)} %bitcast.89, f32[256]{0:T(256)S(1)} %bitcast.88), kind=kLoop, calls=%fused_computation.59 | loop fusion | flops 3145728 | bytes 529920 | tf_op jit(solution)/shard_map/convert_element_type | solution.py:45
  28.0 1.1 convolution_add_fusion.3
  29.1 1.9 %convolution_add_fusion.2 = f32[20,64,128]{2,1,0:T(8,128)} fusion(bf16[256,20,64]{0,2,1:T(8,128)(2,1)S(1)} %bitcast.75, f32[256,20]{0,1:T(8,128)} %get-tuple-element.72, f32[20,64,128]{2,1,0:T(8,128)S(1)} %convolution_add_fusion.3, f32[20]{0:T(128)} %exp.65, bf16[512,256]{1,0:T(8,128)(2,1)S(1)} %divide_convert_fusion.1), kind=kOutput, calls=%fused_computation.43 | convolution fusion | flops 85196800 | bytes 2052176 | tf_op jit(solution)/shard_map/jhp,js->hps/dot_general | solution.py:61
  31.1 1.2 dynamic-slice
  33.0 0.9 dynamic-update-slice
  33.8 10.1 %all-reduce = f32[80]{0:T(128)S(1)} all-reduce(f32[80]{0:T(128)S(1)} %dynamic-update-slice), channel_id=2, replica_groups=mesh['groups'=2,'seq'=4,'tensor'=4] {'seq'}, use_global_device_ids=true, to_apply=%add | all-reduce | flops 80 | bytes 640
  44.1 0.7 mul.319
  44.8 0.7 mul.320
  45.4 0.7 compare_and_fusion
  46.5 3.7 %fusion.18 = f32[256,20,64]{0,2,1:T(8,128)} fusion(bf16[256,20,64]{0,2,1:T(8,128)(2,1)S(1)} %bitcast.78, f32[20,256]{1,0:T(8,128)} %get-tuple-element.70, f32[256,256]{1,0:T(8,128)S(1)} %fusion.57, f32[20,256]{1,0:T(8,128)} %bitcast.81, pred[256,256]{1,0:T(8,128)(4,1)S(1)} %iota_compare_fusion), kind=kOutput, calls=%fused_computation.31 | convolution fusion | flops 175636480 | bytes 2334720 | tf_op jit(solution)/shard_map/hij,jhp->ihp/dot_general | solution.py:58
  50.3 2.9 %fusion.17 = f32[256,20,64]{0,2,1:T(8,128)} fusion(bf16[256,20,64]{0,2,1:T(8,128)(2,1)S(1)} %bitcast.76, f32[20,256]{1,0:T(8,128)S(1)} %copy-done.11, f32[256,256]{1,0:T(8,128)S(1)} %fusion.53, f32[20,256]{1,0:T(8,128)S(1)} %bitcast.84, pred[256,256]{1,0:T(8,128)(4,1)S(1)} %iota_compare_fusion), kind=kOutput, calls=%fused_computation.30 | convolution fusion | flops 175636480 | bytes 2334720 | tf_op jit(solution)/shard_map/hij,jhp->ihp/dot_general | solution.py:58
  53.1 33.0 %all-gather.7.cloned.1.call-done = f32[80,64,128]{2,1,0:T(8,128)} async-done(((f32[20,64,128]{2,1,0:T(8,128)}), f32[80,64,128]{2,1,0:T(8,128)}) %all-gather.7.cloned.1.call-update) | async-done | bytes 2621456 | tf_op jit(solution)/shard_map/all_gather | solution.py:21
  86.3 0.3 fusion.44
  86.6 0.4 copy-done.9
  87.0 0.6 copy-done.3
  87.6 1.4 fusion.21
  89.0 2.8 %copy.40 = f32[256,1280]{1,0:T(8,128)} copy(f32[256,1280]{0,1:T(8,128)} %bitcast.73) | data formatting | bytes 2621440 | tf_op jit(solution)/shard_map/concatenate | solution.py:135
  91.8 0.4 fusion.41
  92.2 0.9 copy-done.2
  93.1 1.4 fusion.22
  94.6 2.9 %copy.41 = f32[256,1280]{1,0:T(8,128)} copy(f32[256,1280]{0,1:T(8,128)} %bitcast.72) | data formatting | bytes 2621440 | tf_op jit(solution)/shard_map/concatenate | solution.py:135
  97.5 4.2 %multiply_reduce_fusion = (f32[512]{0:T(512)S(1)}, f32[512,1280]{1,0:T(8,128)}) fusion(bf16[512,1280]{1,0:T(8,128)(2,1)} %param.16, bf16[512,1280]{1,0:T(8,128)(2,1)S(1)} %divide_convert_fusion, f32[1280]{0:T(1024)S(1)} %copy-done.10, f32[256,1280]{1,0:T(8,128)} %copy.41, f32[256,1280]{1,0:T(8,128)S(1)} %copy-done.1), kind=kLoop, calls=%fused_computation.14 | loop fusion | flops 7208448 | bytes 7871488 | tf_op jit(solution)/shard_map/reduce_sum | solution.py:139
  101.7 6.4 %psum.7 = f32[512]{0:T(512)S(1)} all-reduce(f32[512]{0:T(512)S(1)} %get-tuple-element.66), channel_id=1, replica_groups=mesh['groups'=2,'seq'=4,'tensor'=4] {'tensor'}, use_global_device_ids=true, to_apply=%region_7.8 | all-reduce | flops 512 | bytes 4096 | tf_op jit(solution)/shard_map/psum | solution.py:139
  108.1 2.0 %multiply_convert_fusion.4 = bf16[512,1280]{1,0:T(8,128)(2,1)S(1)} fusion(f32[512,1280]{1,0:T(8,128)} %get-tuple-element.67, f32[1280]{0:T(1024)S(1)} %copy-done.12, f32[512]{0:T(512)S(1)} %add_rsqrt_fusion), kind=kLoop, calls=%fused_computation.13 | loop fusion | flops 1966080 | bytes 3939328 | tf_op jit(solution)/shard_map/convert_element_type | solution.py:143
  110.2 0.9 gather_fusion
  111.1 0.8 broadcast_select_fusion
  112.0 0.2 reshape.192
  112.3 34.4 %all-gather.5.cloned.1.call-done = bf16[512,1280]{1,0:T(8,128)(2,1)} async-done(((bf16[128,1280]{1,0:T(8,128)(2,1)}), bf16[512,1280]{1,0:T(8,128)(2,1)}) %all-gather.5.cloned.1.call-update) | async-done | bytes 1310736 | tf_op jit(solution)/shard_map/all_gather | solution.py:151
  146.7 1.6 %copy.42 = bf16[512,1280]{0,1:T(8,128)(2,1)S(1)} copy(bf16[512,1280]{1,0:T(8,128)(2,1)} %all-gather.5.cloned.1.call-done) | data formatting | bytes 2621440 | tf_op jit(solution)/shard_map/all_gather | solution.py:151
  148.3 0.4 fusion.73
  148.7 0.3 fusion.31
  149.0 0.6 fusion.28
  149.7 0.8 reshape.193
  (68 shorter events, 1.7 us)
Async XLA Ops:
  7.2 79.0 %all-gather.7.cloned.1.call-start = ((), (), s32[]{:S(2)}) async-start(), calls=%async_computation.1 | async-start | bytes 3276800 | tf_op jit(solution)/shard_map/all_gather | solution.py:21
  8.7 12.8 %collective-permute-start = (bf16[3,1536]{1,0:T(4,128)(2,1)S(1)}, bf16[3,1536]{1,0:T(4,128)(2,1)S(1)}, u32[]{:S(2)}, u32[]{:S(2)}) collective-permute-start(bf16[3,1536]{1,0:T(4,128)(2,1)S(1)} %pad_maximum_fusion.2), channel_id=1, source_target_pairs={{0,4},{4,8},{8,12},{1,5},{5,9},{9,13},{2,6},{6,10},{10,14},{3,7},{... | collective-permute-start | bytes 27656 | tf_op jit(solution)/shard_map/ppermute | solution.py:16
  15.3 6.1 %copy-start.4 = (f32[3,8,2,128]{3,1,2,0:T(8,128)}, f32[3,8,2,128]{3,1,2,0:T(8,128)S(1)}, u32[]{:S(2)}) copy-start(f32[3,8,2,128]{3,1,2,0:T(8,128)S(1)} %copy.45) | copy-start | bytes 73732
  16.3 5.1 %copy-start.5 = (f32[3,8,2,128]{3,1,2,0:T(8,128)}, f32[3,8,2,128]{3,1,2,0:T(8,128)S(1)}, u32[]{:S(2)}) copy-start(f32[3,8,2,128]{3,1,2,0:T(8,128)S(1)} %copy.46) | copy-start | bytes 73732
  31.0 115.7 %all-gather.5.cloned.1.call-start = ((), (), s32[]{:S(2)}) async-start(), calls=%async_computation | async-start | bytes 1638400 | tf_op jit(solution)/shard_map/all_gather | solution.py:151
  46.5 3.7 %copy-start.6 = (f32[3,8,2,128]{3,1,2,0:T(8,128)S(1)}, f32[3,8,2,128]{3,1,2,0:T(8,128)}, u32[]{:S(2)}) copy-start(f32[3,8,2,128]{3,1,2,0:T(8,128)} %copy-done.5) | copy-start | bytes 73732
  46.5 3.7 %copy-start.11 = (f32[20,256]{1,0:T(8,128)S(1)}, f32[20,256]{1,0:T(8,128)}, u32[]{:S(2)}) copy-start(f32[20,256]{1,0:T(8,128)} %get-tuple-element.73) | copy-start | bytes 61444
  86.3 0.7 copy-start.9
  86.3 1.3 copy-start.3
  87.6 4.2 %copy-start.13 = (f32[20]{0:T(128)S(1)}, f32[20]{0:T(128)}, u32[]{:S(2)}) copy-start(f32[20]{0:T(128)} %get-tuple-element.84) | copy-start | bytes 244
  89.0 3.2 %copy-start.8 = (f32[256,20]{0,1:T(8,128)S(1)}, f32[256,20]{0,1:T(8,128)}, u32[]{:S(2)}) copy-start(f32[256,20]{0,1:T(8,128)} %get-tuple-element.76) | copy-start | bytes 61444
  91.8 1.3 copy-start.2
  94.6 2.9 %copy-start.1 = (f32[256,1280]{1,0:T(8,128)S(1)}, f32[256,1280]{1,0:T(8,128)}, u32[]{:S(2)}) copy-start(f32[256,1280]{1,0:T(8,128)} %copy.40) | copy-start | bytes 3932164
  94.6 2.9 %copy-start.10 = (f32[1280]{0:T(1024)S(1)}, f32[1280]{0:T(1024)}, u32[]{:S(2)}) copy-start(f32[1280]{0:T(1024)} %mul.320) | copy-start | bytes 15364
  97.5 10.6 %copy-start.12 = (f32[1280]{0:T(1024)S(1)}, f32[1280]{0:T(1024)}, u32[]{:S(2)}) copy-start(f32[1280]{0:T(1024)} %param.23) | copy-start | bytes 15364
  110.1 38.2 %copy-start = (bf16[512,1280]{1,0:T(8,128)(2,1)}, bf16[512,1280]{1,0:T(8,128)(2,1)S(1)}, u32[]{:S(2)}) copy-start(bf16[512,1280]{1,0:T(8,128)(2,1)S(1)} %multiply_convert_fusion.4) | copy-start | bytes 3932164
  110.2 1.8 %copy-start.7 = (bf16[40,1280]{1,0:T(8,128)(2,1)S(1)}, bf16[40,1280]{1,0:T(8,128)(2,1)}, u32[]{:S(2)}) copy-start(bf16[40,1280]{1,0:T(8,128)(2,1)} %param.25) | copy-start | bytes 307204
  110.2 2.0 %copy-start.14 = (s32[40]{0:T(128)S(1)}, s32[40]{0:T(128)}, u32[]{:S(2)}) copy-start(s32[40]{0:T(128)} %param.27) | copy-start | bytes 484
  110.2 2.0 %copy-start.15 = (s32[40]{0:T(128)S(1)}, s32[40]{0:T(128)}, u32[]{:S(2)}) copy-start(s32[40]{0:T(128)} %param.26) | copy-start | bytes 484
Sparse Core Ops, SparseCore 0:
  31.1 55.0 all-gather.6
  112.1 34.5 all-gather.4
where the time goes:
time: 158 us; the launch traced here: 157 us
  waiting for transfers between devices  67.5 us (43%)
  other arithmetic  20 us (13%)
  local copies, waits for them, and re-layouts  18.7 us (12%)
  blocking collectives  16.5 us (10%)
  between operations  15.1 us (10%)
  matrix products  14.5 us (9%)
  starting transfers between devices  5.04 us (3%)
    all_gather x1, waiting for transfers between devices, local(): piece = lax.all_gather(summaries, 'seq', axis=0, tiled=True)  34.4 us
    all_gather x1, waiting for transfers between devices, prefix(): gathered = jax.tree.map(lambda a: lax.all_gather(a, axis), part)  33 us
    unnamed x1, blocking collectives  10.1 us
    dot_general x2, matrix products, stretch_local(): jnp.einsum('hij,jhp->ihp', mixing, x_block, preferred_element_type=jnp.fl...  6.59 us
    psum x1, blocking collectives, local(): square_sum = lax.psum(jnp.sum(gated * gated, axis=1), 'tensor')  6.37 us
    convert_element_type x2, other arithmetic, causal_conv(): return silu_act(summed).astype(jnp.bfloat16)  5.91 us
    concatenate x2, local copies, waits for them, and re-layouts, local(): jnp.concatenate(pieces_out, axis=0)  5.7 us
    ppermute x1, starting transfers between devices, passed_along(): lax.ppermute(value, axis, [(source, source + steps) for source in range(l...  4.96 us
  transfers between devices with their start and end apart: 3, of which 2 were waited for; matrix products, arithmetic and copies ran while one was open for 12% of the time, Pallas kernels for 0%

commit v1 on v0

--- a/solution.py
+++ b/solution.py
@@ -148,7 +148,18 @@
     scale_factor = 1.0 / math.sqrt(pool_width)
     pools_local = pool_query.shape[0]
     queries = pool_query.reshape(pools_local, pool_heads_local, pool_width)
-    piece = lax.all_gather(summaries, "seq", axis=0, tiled=True)
+    res, local_part, now = (lax.axis_size("seq"), lax.axis_index("seq"), summaries.shape[0])
+    mixed_arr, formed = (summaries, 1)
+    while formed < res:
+        mixed_arr = jnp.concatenate(
+            [
+                mixed_arr,
+                lax.ppermute(mixed_arr, "seq", [(nth, (nth - formed) % res) for nth in range(res)]),
+            ],
+            axis=0,
+        )
+        formed = 2 * formed
+    piece = jnp.roll(mixed_arr, shift=local_part * now, axis=0)
     peak = jnp.full((pool_heads_local, pools_local), MASKED, jnp.float32)
     numer = jnp.zeros((pools_local, pool_heads_local, pool_width), jnp.float32)
     count = piece.shape[0]

time: 158 us -> 168 us (1.063)
  starting transfers between devices: 5.04 us -> 11.6 us
  local copies, waits for them, and re-layouts: 18.7 us -> 23.2 us
  waiting for transfers between devices: 67.5 us -> 65.2 us
    all_gather x1 -> x0, waiting for transfers between devices: 34.4 us -> none  [local(): piece = lax.all_gather(summaries, 'seq', axis=0, tiled=True)]
    ppermute x0 -> x2, waiting for transfers between devices: none -> 32.1 us  [local(): lax.ppermute(mixed_arr, 'seq', [(nth, (nth - formed) % res) for nth in ra...]
    ppermute x0 -> x2, starting transfers between devices: none -> 6.57 us  [local(): lax.ppermute(mixed_arr, 'seq', [(nth, (nth - formed) % res) for nth in ra...]
    unnamed x39 -> x41, local copies, waits for them, and re-layouts: 4.11 us -> 7.25 us
    dynamic_slice x0 -> x2, local copies, waits for them, and re-layouts: none -> 2.05 us  [local(): piece = jnp.roll(mixed_arr, shift=local_part * now, axis=0)]
  transfers between devices with their start and end apart: 3 -> 4, of which waited for: 2 -> 3; matrix products, arithmetic and copies ran while one was open for 12% -> 12% of each run, Pallas kernels for 0% -> 0%
where the time goes in v1:
time: 168 us; the launch traced here: 167 us
  waiting for transfers between devices  65.2 us (39%)
  local copies, waits for them, and re-layouts  23.2 us (14%)
  other arithmetic  20.7 us (12%)
  blocking collectives  16.5 us (10%)
  between operations  15.1 us (9%)
  matrix products  14.5 us (9%)
  starting transfers between devices  11.6 us (7%)
    all_gather x1, waiting for transfers between devices, prefix(): gathered = jax.tree.map(lambda a: lax.all_gather(a, axis), part)  33.1 us
    ppermute x2, waiting for transfers between devices, local(): lax.ppermute(mixed_arr, 'seq', [(nth, (nth - formed) % res) for nth in ra...  32.1 us
    unnamed x1, blocking collectives  10.1 us
    unnamed x41, local copies, waits for them, and re-layouts  7.25 us
    dot_general x2, matrix products, stretch_local(): jnp.einsum('hij,jhp->ihp', mixing, x_block, preferred_element_type=jnp.fl...  6.59 us
    ppermute x2, starting transfers between devices, local(): lax.ppermute(mixed_arr, 'seq', [(nth, (nth - formed) % res) for nth in ra...  6.57 us
    psum x1, blocking collectives, local(): square_sum = lax.psum(jnp.sum(gated * gated, axis=1), 'tensor')  6.37 us
    convert_element_type x2, other arithmetic, causal_conv(): return silu_act(summed).astype(jnp.bfloat16)  5.91 us
  transfers between devices with their start and end apart: 4, of which 3 were waited for; matrix products, arithmetic and copies ran while one was open for 12% of the time, Pallas kernels for 0%

profile of v1, /device:TPU:0, one launch (start us, length us, event | category | flops | bytes accessed | tf_op | source)
XLA Modules:
  0.0 166.8 jit_solution(15728839836271906276)
XLA Ops:
  7.2 0.7 slice.120
  7.9 0.7 slice.121
  8.7 5.0 %collective-permute-start = (bf16[3,1536]{1,0:T(4,128)(2,1)S(1)}, bf16[3,1536]{1,0:T(4,128)(2,1)S(1)}, u32[]{:S(2)}, u32[]{:S(2)}) collective-permute-start(bf16[3,1536]{1,0:T(4,128)(2,1)S(1)} %pad_maximum_fusion.3), channel_id=1, source_target_pairs={{0,4},{4,8},{8,12},{1,5},{5,9},{9,13},{2,6},{6,10},{10,14},{3,7},{... | collective-permute-start | bytes 27656 | tf_op jit(solution)/shard_map/ppermute | solution.py:16
  13.6 0.8 fusion.71
  14.4 0.6 reduce-window.14
  15.4 0.6 reduce-window.16
  16.3 0.8 slice_convert_fusion.3
  17.2 0.8 slice_reduce_fusion.2
  18.5 1.5 fusion.70
  19.9 0.9 convert_reduce_fusion.3
  20.8 0.6 exp.65
  21.5 4.0 %divide_convert_fusion = bf16[512,1280]{1,0:T(8,128)(2,1)S(1)} fusion(bf16[512,1280]{1,0:T(8,128)(2,1)} %param.15, bf16[3,1280]{1,0:T(4,128)(2,1)S(1)} %slice.158, f32[1280]{0:T(1024)S(1)} %get-tuple-element.52, f32[1280]{0:T(1024)S(1)} %get-tuple-element.53, f32[1280]{0:T(1024)S(1)} %get-tuple-element.51, f32[1280]{0:T(1024)S(1)} %get-tuple-element.50), kind=kLoop, calls=%fused_computation.25 | loop fusion | flops 15728640 | bytes 2649600 | tf_op jit(solution)/shard_map/convert_element_type | solution.py:45
  26.1 1.9 %divide_convert_fusion.1 = bf16[512,256]{1,0:T(8,128)(2,1)S(1)} fusion(bf16[512,256]{1,0:T(8,128)(2,1)} %param.17, bf16[3,256]{1,0:T(4,128)(2,1)S(1)} %slice.165, f32[256]{0:T(256)S(1)} %bitcast.90, f32[256]{0:T(256)S(1)} %bitcast.91, f32[256]{0:T(256)S(1)} %bitcast.89, f32[256]{0:T(256)S(1)} %bitcast.88), kind=kLoop, calls=%fused_computation.60 | loop fusion | flops 3145728 | bytes 529920 | tf_op jit(solution)/shard_map/convert_element_type | solution.py:45
  28.0 1.1 convolution_add_fusion.3
  29.1 1.9 %convolution_add_fusion.2 = f32[20,64,128]{2,1,0:T(8,128)} fusion(bf16[256,20,64]{0,2,1:T(8,128)(2,1)S(1)} %bitcast.75, f32[256,20]{0,1:T(8,128)} %get-tuple-element.74, f32[20,64,128]{2,1,0:T(8,128)S(1)} %convolution_add_fusion.3, f32[20]{0:T(128)} %exp.65, bf16[512,256]{1,0:T(8,128)(2,1)S(1)} %divide_convert_fusion.1), kind=kOutput, calls=%fused_computation.43 | convolution fusion | flops 85196800 | bytes 2052176 | tf_op jit(solution)/shard_map/jhp,js->hps/dot_general | solution.py:61
  31.0 1.2 dynamic-slice
  32.9 0.9 dynamic-update-slice
  33.8 10.1 %all-reduce = f32[80]{0:T(128)S(1)} all-reduce(f32[80]{0:T(128)S(1)} %dynamic-update-slice), channel_id=2, replica_groups=mesh['groups'=2,'seq'=4,'tensor'=4] {'seq'}, use_global_device_ids=true, to_apply=%add | all-reduce | flops 80 | bytes 640
  44.0 0.7 mul.322
  44.7 0.7 mul.323
  45.4 0.7 compare_and_fusion
  46.5 3.7 %fusion.18 = f32[256,20,64]{0,2,1:T(8,128)} fusion(bf16[256,20,64]{0,2,1:T(8,128)(2,1)S(1)} %bitcast.78, f32[20,256]{1,0:T(8,128)} %get-tuple-element.72, f32[256,256]{1,0:T(8,128)S(1)} %fusion.57, f32[20,256]{1,0:T(8,128)} %bitcast.81, pred[256,256]{1,0:T(8,128)(4,1)S(1)} %iota_compare_fusion), kind=kOutput, calls=%fused_computation.31 | convolution fusion | flops 175636480 | bytes 2334720 | tf_op jit(solution)/shard_map/hij,jhp->ihp/dot_general | solution.py:58
  50.2 2.9 %fusion.17 = f32[256,20,64]{0,2,1:T(8,128)} fusion(bf16[256,20,64]{0,2,1:T(8,128)(2,1)S(1)} %bitcast.76, f32[20,256]{1,0:T(8,128)S(1)} %copy-done.11, f32[256,256]{1,0:T(8,128)S(1)} %fusion.53, f32[20,256]{1,0:T(8,128)S(1)} %bitcast.84, pred[256,256]{1,0:T(8,128)(4,1)S(1)} %iota_compare_fusion), kind=kOutput, calls=%fused_computation.30 | convolution fusion | flops 175636480 | bytes 2334720 | tf_op jit(solution)/shard_map/hij,jhp->ihp/dot_general | solution.py:58
  53.1 33.1 %all-gather.4.cloned.1.call-done = f32[80,64,128]{2,1,0:T(8,128)} async-done(((f32[20,64,128]{2,1,0:T(8,128)}), f32[80,64,128]{2,1,0:T(8,128)}) %all-gather.4.cloned.1.call-update) | async-done | bytes 2621456 | tf_op jit(solution)/shard_map/all_gather | solution.py:21
  87.0 0.6 copy-done.3
  87.6 1.4 fusion.21
  89.0 2.8 %copy.40 = f32[256,1280]{1,0:T(8,128)} copy(f32[256,1280]{0,1:T(8,128)} %bitcast.73) | data formatting | bytes 2621440 | tf_op jit(solution)/shard_map/concatenate | solution.py:135
  92.2 0.9 copy-done.2
  93.1 1.4 fusion.22
  94.6 2.9 %copy.41 = f32[256,1280]{1,0:T(8,128)} copy(f32[256,1280]{0,1:T(8,128)} %bitcast.72) | data formatting | bytes 2621440 | tf_op jit(solution)/shard_map/concatenate | solution.py:135
  97.5 4.2 %multiply_reduce_fusion = (f32[512]{0:T(512)S(1)}, f32[512,1280]{1,0:T(8,128)}) fusion(bf16[512,1280]{1,0:T(8,128)(2,1)} %param.16, bf16[512,1280]{1,0:T(8,128)(2,1)S(1)} %divide_convert_fusion, f32[1280]{0:T(1024)S(1)} %copy-done.10, f32[256,1280]{1,0:T(8,128)} %copy.41, f32[256,1280]{1,0:T(8,128)S(1)} %copy-done.1), kind=kLoop, calls=%fused_computation.14 | loop fusion | flops 7208448 | bytes 7871488 | tf_op jit(solution)/shard_map/reduce_sum | solution.py:139
  101.7 6.4 %psum.7 = f32[512]{0:T(512)S(1)} all-reduce(f32[512]{0:T(512)S(1)} %get-tuple-element.68), channel_id=1, replica_groups=mesh['groups'=2,'seq'=4,'tensor'=4] {'tensor'}, use_global_device_ids=true, to_apply=%region_7.8 | all-reduce | flops 512 | bytes 4096 | tf_op jit(solution)/shard_map/psum | solution.py:139
  108.1 2.0 %multiply_convert_fusion.4 = bf16[512,1280]{1,0:T(8,128)(2,1)S(1)} fusion(f32[512,1280]{1,0:T(8,128)} %get-tuple-element.69, f32[1280]{0:T(1024)S(1)} %copy-done.12, f32[512]{0:T(512)S(1)} %add_rsqrt_fusion), kind=kLoop, calls=%fused_computation.13 | loop fusion | flops 1966080 | bytes 3939328 | tf_op jit(solution)/shard_map/convert_element_type | solution.py:143
  110.2 0.9 gather_fusion
  111.1 0.8 constant_dynamic-update-slice_fusion.5
  111.9 5.3 %collective-permute-start.1 = (bf16[128,1280]{1,0:T(8,128)(2,1)S(1)}, bf16[128,1280]{1,0:T(8,128)(2,1)S(1)}, u32[]{:S(2)}, u32[]{:S(2)}) collective-permute-start(bf16[128,1280]{1,0:T(8,128)(2,1)S(1)} %get-tuple-element.65), channel_id=1, source_target_pairs={{0,12},{4,0},{8,4},{12,8},{1,13},{5,1},{9,5},{13,9},{2,14},{6,2},{... | collective-permute-start | bytes 983048 | tf_op jit(solution)/shard_map/ppermute | solution.py:157
  117.2 5.9 %collective-permute-done.1 = bf16[128,1280]{1,0:T(8,128)(2,1)S(1)} collective-permute-done((bf16[128,1280]{1,0:T(8,128)(2,1)S(1)}, bf16[128,1280]{1,0:T(8,128)(2,1)S(1)}, u32[]{:S(2)}, u32[]{:S(2)}) %collective-permute-start.1) | collective-permute-done | bytes 327712 | tf_op jit(solution)/shard_map/ppermute | solution.py:157
  123.2 1.2 collective-permute-start.2
  124.7 0.7 fusion.46
  125.5 0.7 constant_dynamic-update-slice_fusion.4
  126.2 26.1 %collective-permute-done.2 = bf16[256,1280]{1,0:T(8,128)(2,1)S(1)} collective-permute-done((bf16[256,1280]{1,0:T(8,128)(2,1)S(1)}, bf16[256,1280]{1,0:T(8,128)(2,1)S(1)}, u32[]{:S(2)}, u32[]{:S(2)}) %collective-permute-start.2) | collective-permute-done | bytes 655392 | tf_op jit(solution)/shard_map/ppermute | solution.py:157
  152.3 0.9 constant_dynamic-update-slice_fusion.3
  153.2 0.8 constant_dynamic-update-slice_fusion.2
  154.0 0.7 constant_dynamic-update-slice_fusion.1
  154.7 0.9 constant_dynamic-update-slice_fusion
  155.6 1.4 constant_dynamic-slice_fusion
  157.0 0.7 copy.42
  159.1 0.8 reshape.193
  (74 shorter events, 5.2 us)
Async XLA Ops:
  7.2 79.0 %all-gather.4.cloned.1.call-start = ((), (), s32[]{:S(2)}) async-start(), calls=%async_computation | async-start | bytes 3276800 | tf_op jit(solution)/shard_map/all_gather | solution.py:21
  8.7 12.8 %collective-permute-start = (bf16[3,1536]{1,0:T(4,128)(2,1)S(1)}, bf16[3,1536]{1,0:T(4,128)(2,1)S(1)}, u32[]{:S(2)}, u32[]{:S(2)}) collective-permute-start(bf16[3,1536]{1,0:T(4,128)(2,1)S(1)} %pad_maximum_fusion.3), channel_id=1, source_target_pairs={{0,4},{4,8},{8,12},{1,5},{5,9},{9,13},{2,6},{6,10},{10,14},{3,7},{... | collective-permute-start | bytes 27656 | tf_op jit(solution)/shard_map/ppermute | solution.py:16
  15.3 6.1 %copy-start.4 = (f32[3,8,2,128]{3,1,2,0:T(8,128)}, f32[3,8,2,128]{3,1,2,0:T(8,128)S(1)}, u32[]{:S(2)}) copy-start(f32[3,8,2,128]{3,1,2,0:T(8,128)S(1)} %copy.45) | copy-start | bytes 73732
  16.3 5.1 %copy-start.5 = (f32[3,8,2,128]{3,1,2,0:T(8,128)}, f32[3,8,2,128]{3,1,2,0:T(8,128)S(1)}, u32[]{:S(2)}) copy-start(f32[3,8,2,128]{3,1,2,0:T(8,128)S(1)} %copy.46) | copy-start | bytes 73732
  46.5 3.7 %copy-start.6 = (f32[3,8,2,128]{3,1,2,0:T(8,128)S(1)}, f32[3,8,2,128]{3,1,2,0:T(8,128)}, u32[]{:S(2)}) copy-start(f32[3,8,2,128]{3,1,2,0:T(8,128)} %copy-done.5) | copy-start | bytes 73732
  46.5 3.7 %copy-start.11 = (f32[20,256]{1,0:T(8,128)S(1)}, f32[20,256]{1,0:T(8,128)}, u32[]{:S(2)}) copy-start(f32[20,256]{1,0:T(8,128)} %get-tuple-element.75) | copy-start | bytes 61444
  86.3 0.7 copy-start.9
  86.3 1.3 copy-start.3
  87.6 4.2 %copy-start.13 = (f32[20]{0:T(128)S(1)}, f32[20]{0:T(128)}, u32[]{:S(2)}) copy-start(f32[20]{0:T(128)} %get-tuple-element.86) | copy-start | bytes 244
  89.0 3.2 %copy-start.8 = (f32[256,20]{0,1:T(8,128)S(1)}, f32[256,20]{0,1:T(8,128)}, u32[]{:S(2)}) copy-start(f32[256,20]{0,1:T(8,128)} %get-tuple-element.78) | copy-start | bytes 61444
  91.8 1.3 copy-start.2
  94.6 2.9 %copy-start.1 = (f32[256,1280]{1,0:T(8,128)S(1)}, f32[256,1280]{1,0:T(8,128)}, u32[]{:S(2)}) copy-start(f32[256,1280]{1,0:T(8,128)} %copy.40) | copy-start | bytes 3932164
  94.6 2.9 %copy-start.10 = (f32[1280]{0:T(1024)S(1)}, f32[1280]{0:T(1024)}, u32[]{:S(2)}) copy-start(f32[1280]{0:T(1024)} %mul.323) | copy-start | bytes 15364
  97.5 10.6 %copy-start.12 = (f32[1280]{0:T(1024)S(1)}, f32[1280]{0:T(1024)}, u32[]{:S(2)}) copy-start(f32[1280]{0:T(1024)} %param.23) | copy-start | bytes 15364
  110.1 13.1 %copy-start = (bf16[512,1280]{1,0:T(8,128)(2,1)}, bf16[512,1280]{1,0:T(8,128)(2,1)S(1)}, u32[]{:S(2)}) copy-start(bf16[512,1280]{1,0:T(8,128)(2,1)S(1)} %multiply_convert_fusion.4) | copy-start | bytes 3932164
  110.2 14.3 %copy-start.7 = (bf16[40,1280]{1,0:T(8,128)(2,1)S(1)}, bf16[40,1280]{1,0:T(8,128)(2,1)}, u32[]{:S(2)}) copy-start(bf16[40,1280]{1,0:T(8,128)(2,1)} %param.25) | copy-start | bytes 307204
  110.2 14.5 %copy-start.14 = (s32[40]{0:T(128)S(1)}, s32[40]{0:T(128)}, u32[]{:S(2)}) copy-start(s32[40]{0:T(128)} %param.27) | copy-start | bytes 484
  111.9 11.3 %collective-permute-start.1 = (bf16[128,1280]{1,0:T(8,128)(2,1)S(1)}, bf16[128,1280]{1,0:T(8,128)(2,1)S(1)}, u32[]{:S(2)}, u32[]{:S(2)}) collective-permute-start(bf16[128,1280]{1,0:T(8,128)(2,1)S(1)} %get-tuple-element.65), channel_id=1, source_target_pairs={{0,12},{4,0},{8,4},{12,8},{1,13},{5,1},{9,5},{13,9},{2,14},{6,2},{... | collective-permute-start | bytes 983048 | tf_op jit(solution)/shard_map/ppermute | solution.py:157
  123.2 29.1 %collective-permute-start.2 = (bf16[256,1280]{1,0:T(8,128)(2,1)S(1)}, bf16[256,1280]{1,0:T(8,128)(2,1)S(1)}, u32[]{:S(2)}, u32[]{:S(2)}) collective-permute-start(bf16[256,1280]{1,0:T(8,128)(2,1)S(1)} %pad_maximum_fusion.1), channel_id=1, source_target_pairs={{0,8},{4,12},{8,0},{12,4},{1,9},{5,13},{9,1},{13,5},{2,10},{6,14},... | collective-permute-start | bytes 1966088 | tf_op jit(solution)/shard_map/ppermute | solution.py:157
Sparse Core Ops, SparseCore 0:
  31.1 55.0 all-gather.3
